TPU v7x, 512 devices: a whole 4x8x8 slice. The times are simulated.
512 devices in a mesh: slab: 64 (over z, x, core), obs: 8 (over y).
Axes of the slice: x: 4, y: 8, z: 8, core: 2. Of those that a mesh axis runs over, the one named last changes fastest.
Arguments:
- background_members: float32 [64, 1048576], P('slab', 'obs'), may hold values from -6 to 6
- measurement_jitter: bfloat16 [64, 8, 65536], P(None, 'obs', 'slab'), may hold values from -5 to 5
- measurement_readings: float32 [8, 65536], P('obs', 'slab'), may hold values from -8 to 8
- measurement_noise_spread: float32 [8, 65536], P('obs', 'slab'), may hold values from 0.2 to 2
- measurement_grid_location: int32 [8, 65536], P('obs', 'slab'), may hold values from 0 to 2047
- active_tallies: int32 [8, 64], P('obs', 'slab'), may hold values from 128 to 1024, as said below
- coupling_listing: int32 [8, 2048, 8], P('obs', 'slab'), may hold values from 0 to 63, as said below
- taper_factors: float32 [8, 2048, 8], P('obs', 'slab'), may hold values from 0.1 to 1
Outputs:
- analysis: float32 [64, 1048576], P('slab', 'obs')
Inputs may be any that keep to these rules, and one draw needn't show every extreme that they name: `active_tallies`: some region of some group holds 1024 live observations; slots beyond a region's count are padding. `coupling_listing`: the 8 observation blocks listed for a state block are distinct.
All inputs are finite; a program needn't handle non-finite values.
Results may differ from a plain program's by a relative error of at most 0.0063.
Values may be sent and summed in bfloat16 or wider, within the bound.
No kernel may reach another device: no remote copies, remote signals or barrier semaphores. Data moves between devices by JAX's collectives and lax.ppermute only.
A program may use at most 64 MiB of HBM per device.

v0:
```python
import math
import jax
import jax.numpy as jnp
from jax import lax
from jax.sharding import PartitionSpec as P

OB = 128
highest = lax.Precision.HIGHEST


def compute_increment(
    tile_work,
    measurement_jitter,
    measurement_readings,
    measurement_noise_spread,
    measurement_grid_location,
    active_tallies,
    coupling_listing,
    taper_factors,
):
    members = tile_work.shape[0]
    points = tile_work.shape[1]
    blocks = coupling_listing.shape[1]
    block_width = points // blocks
    deviation = tile_work - jnp.mean(tile_work, axis=0, keepdims=True)
    positions = measurement_grid_location[0]
    obs_count = positions.shape[0]
    prior_value = jnp.take(tile_work, positions, axis=1)
    prior_shift = prior_value - jnp.mean(prior_value, axis=0, keepdims=True)
    spread = jnp.sum(prior_shift * prior_shift, axis=0, keepdims=True) / (members - 1)
    usable = jnp.arange(obs_count, dtype=jnp.int32)[None, :] < active_tallies[0, 0]
    innovation = (
        measurement_readings + measurement_jitter[:, 0, :].astype(jnp.float32) - prior_value
    ) / (spread + measurement_noise_spread)
    gain_input = jnp.where(usable, innovation, jnp.float32(0.0)).astype(jnp.bfloat16)
    prior_low = prior_shift.astype(jnp.bfloat16)
    block_links = coupling_listing[0]
    factor = taper_factors[0] / (members - 1)
    gathered = (
        lax.all_gather(prior_low, "obs", axis=1, tiled=True),
        lax.all_gather(gain_input, "obs", axis=1, tiled=True),
    )
    all_prior = gathered[0].reshape(members, -1, OB)
    all_gain = gathered[1].reshape(members, -1, OB)
    group_size = math.gcd(blocks, 8)
    group_count = blocks // group_size

    def one_group(group_index, running):
        first_block = group_index * group_size
        local_dev = lax.dynamic_slice_in_dim(
            deviation, first_block * block_width, group_size * block_width, 1
        )
        local_dev = local_dev.reshape(members, group_size, block_width)
        chosen = lax.dynamic_slice_in_dim(block_links, first_block, group_size, 0)
        scales = lax.dynamic_slice_in_dim(factor, first_block, group_size, 0)
        picked_prior = jnp.take(all_prior, chosen, axis=1).astype(jnp.float32)
        picked_gain = jnp.take(all_gain, chosen, axis=1).astype(jnp.float32)
        covariance = jnp.einsum("mgp,mglo->glpo", local_dev, picked_prior, precision=highest)
        update = jnp.einsum("glpo,mglo,gl->mgp", covariance, picked_gain, scales, precision=highest)
        update = update.reshape(members, group_size * block_width)
        return lax.dynamic_update_slice_in_dim(running, update, first_block * block_width, 1)

    increment = lax.fori_loop(0, group_count, one_group, jnp.zeros_like(deviation))
    return increment.astype(jnp.bfloat16)


def local(
    background_members,
    measurement_jitter,
    measurement_readings,
    measurement_noise_spread,
    measurement_grid_location,
    active_tallies,
    coupling_listing,
    taper_factors,
):
    grid_segment_piece = lax.all_to_all(
        background_members, "slab", split_axis=1, concat_axis=0, tiled=True
    )
    tile_work = lax.optimization_barrier(grid_segment_piece.astype(jnp.bfloat16)).astype(
        jnp.float32
    )
    reduced_correction = compute_increment(
        tile_work,
        measurement_jitter,
        measurement_readings,
        measurement_noise_spread,
        measurement_grid_location,
        active_tallies,
        coupling_listing,
        taper_factors,
    )
    analysis = grid_segment_piece + lax.optimization_barrier(reduced_correction).astype(jnp.float32)
    return lax.all_to_all(analysis, "slab", split_axis=0, concat_axis=1, tiled=True)


def solution(mesh):
    return jax.shard_map(
        local,
        mesh=mesh,
        in_specs=(
            P("slab", "obs"),
            P(None, "obs", "slab"),
            P("obs", "slab"),
            P("obs", "slab"),
            P("obs", "slab"),
            P("obs", "slab"),
            P("obs", "slab", None),
            P("obs", "slab", None),
        ),
        out_specs=P("slab", "obs"),
        check_vma=False,
    )
```

profile of v0, /device:TPU:1, one launch (start us, length us, event | category | flops | bytes accessed | tf_op | source)
XLA Modules:
  0.0 229.1 jit_solution(7997305621396136883)
XLA Ops:
  6.5 14.8 %all-to-all-start = ((f32[1,64,2048]{2,0,1:T(1,128)}), f32[1,64,2048]{2,0,1:T(1,128)S(1)}, u32[]{:S(2)}, u32[]{:S(2)}) async-start(f32[1,64,2048]{2,0,1:T(1,128)} %bitcast.93), calls=%async_computation | async-start | bytes 1048576 | tf_op jit(solution)/shard_map/all_to_all | solution.py:77
  22.1 1.1 copy.33
  23.1 0.7 iota_compare_fusion
  23.8 0.7 compare_select_fusion.1
  24.5 14.5 %all-to-all-done = f32[1,64,2048]{2,0,1:T(1,128)S(1)} async-done(((f32[1,64,2048]{2,0,1:T(1,128)}), f32[1,64,2048]{2,0,1:T(1,128)S(1)}, u32[]{:S(2)}, u32[]{:S(2)}) %all-to-all-start) | async-done | bytes 524320 | tf_op jit(solution)/shard_map/all_to_all | solution.py:77
  39.1 0.2 copy.51
  39.2 0.7 copy-done
  39.9 0.2 copy.34
  40.1 2.8 %gather_fusion.2 = f32[1024,64]{1,0:T(8,128)S(1)} fusion(f32[64,2048]{0,1:T(8,128)S(1)} %copy.34, s32[1024]{0:T(1024)S(1)} %broadcast_clamp_fusion), kind=kCustom, calls=%fused_computation.2 | custom fusion | bytes 528384 | tf_op jit(solution)/shard_map/jit(_take)/gather | solution.py:28
  43.0 0.4 select_reduce_fusion
  43.3 1.0 fusion.18
  44.4 1.6 fusion.17
  46.1 0.7 all-gather.5.cloned.1.call-update
  46.8 0.1 copy.32
  47.0 0.8 broadcast_subtract_fusion
  47.8 33.9 %all-gather.3.cloned.1.call-done = bf16[64,8192]{0,1:T(8,128)(2,1)} async-done(((bf16[64,1024]{0,1:T(8,128)(2,1)}), bf16[64,8192]{0,1:T(8,128)(2,1)}) %all-gather.3.cloned.1.call-update) | async-done | bytes 1048592 | tf_op jit(solution)/shard_map/all_gather | solution.py:41
  81.7 2.7 %copy.35 = bf16[64,64,128]{2,0,1:T(8,128)(2,1)} copy(bf16[64,64,128]{0,2,1:T(8,128)(2,1)} %bitcast.90) | data formatting | bytes 2097152 | tf_op jit(solution)/shard_map/while | solution.py:63
  84.4 41.5 %all-gather.5.cloned.1.call-done = bf16[64,8192]{0,1:T(8,128)(2,1)} async-done(((bf16[64,1024]{0,1:T(8,128)(2,1)}), bf16[64,8192]{0,1:T(8,128)(2,1)}) %all-gather.5.cloned.1.call-update) | async-done | bytes 1048592 | tf_op jit(solution)/shard_map/all_gather | solution.py:40
  126.0 2.7 %copy.36 = bf16[64,64,128]{2,0,1:T(8,128)(2,1)} copy(bf16[64,64,128]{0,2,1:T(8,128)(2,1)} %bitcast.91) | data formatting | bytes 2097152 | tf_op jit(solution)/shard_map/while | solution.py:63
  128.7 58.3 %while.15 = (s32[]{:T(128)}, bf16[64,2048]{1,0:T(8,128)(2,1)S(1)}, s32[32,8]{1,0:T(8,128)S(1)}, bf16[64,64,128]{2,0,1:T(8,128)(2,1)}, bf16[64,64,128]{2,0,1:T(8,...) while((s32[]{:T(128)}, bf16[64,2048]{1,0:T(8,128)(2,1)S(1)}, ...), condition=%wide.region_4.6_spmd, body=%wide.region_3.5_spmd.sunk | while | flops 809502080 | bytes 13704617 | solution.py:63
  128.7 0.1 reshape.156
  128.8 2.0 gather_fusion
  130.8 0.9 constant_dynamic-slice_fusion.2
  131.7 0.1 copy.58
  131.9 2.4 %fusion.36 = f32[8,8,128,64]{2,3,1,0:T(8,128)} fusion(f32[64,8,64,1]{0,2,3,1:T(8,128)S(1)} %bitcast.85, bf16[8,8,64,128]{3,2,1,0:T(8,128)(2,1)S(1)} %bitcast.83, pred[8,8]{1,0:T(8,128)(4,1)S(1)} %get-tuple-element.277), kind=kOutput, calls=%fused_computation.6.clone.1 | convolution fusion | flops 403177472 | bytes 3276864 | tf_op jit(solution)/shard_map/while/body/eval_jaxpr/mgp,mglo->glpo/dot_general | solution.py:58
  134.2 2.0 gather_fusion.1
  136.2 3.4 %convolution_bitcast_fusion.2 = f32[64,8,8,64]{3,0,2,1:T(8,128)S(1)} fusion(f32[8,8,128,64]{2,3,1,0:T(8,128)} %fusion.36, bf16[8,8,64,128]{3,2,1,0:T(8,128)(2,1)S(1)} %bitcast.84, pred[8,8]{1,0:T(8,128)(4,1)S(1)} %get-tuple-element.277), kind=kOutput, calls=%fused_computation.5.clone.1 | convolution fusion | flops 403177472 | bytes 4194368 | tf_op jit(solution)/shard_map/while/body/eval_jaxpr/glpo,mglo,gl->mgp/dot_general | solution.py:59
  139.8 3.1 %fusion.37 = bf16[8,1,64,64]{3,1,2,0:T(2,128)(2,1)S(1)} fusion(f32[8,8,1,1]{1,2,3,0:T(1,128)S(1)} %copy.57, f32[64,8,8,64]{3,0,2,1:T(8,128)S(1)} %convolution_bitcast_fusion.2), kind=kOutput, calls=%fused_computation.3.clone.1 | convolution fusion | flops 3145728 | bytes 1114368 | tf_op jit(solution)/shard_map/while/body/eval_jaxpr/glpo,mglo,gl->mgp/dot_general | solution.py:59
  142.9 0.2 copy.59
  143.1 0.1 reshape.157
  143.3 0.1 reshape.156
  143.4 2.0 gather_fusion
  145.4 0.9 constant_dynamic-slice_fusion.2
  146.3 0.1 copy.58
  146.4 2.4 %fusion.36 = f32[8,8,128,64]{2,3,1,0:T(8,128)} fusion(f32[64,8,64,1]{0,2,3,1:T(8,128)S(1)} %bitcast.85, bf16[8,8,64,128]{3,2,1,0:T(8,128)(2,1)S(1)} %bitcast.83, pred[8,8]{1,0:T(8,128)(4,1)S(1)} %get-tuple-element.277), kind=kOutput, calls=%fused_computation.6.clone.1 | convolution fusion | flops 403177472 | bytes 3276864 | tf_op jit(solution)/shard_map/while/body/eval_jaxpr/mgp,mglo->glpo/dot_general | solution.py:58
  148.8 2.0 gather_fusion.1
  150.8 3.4 %convolution_bitcast_fusion.2 = f32[64,8,8,64]{3,0,2,1:T(8,128)S(1)} fusion(f32[8,8,128,64]{2,3,1,0:T(8,128)} %fusion.36, bf16[8,8,64,128]{3,2,1,0:T(8,128)(2,1)S(1)} %bitcast.84, pred[8,8]{1,0:T(8,128)(4,1)S(1)} %get-tuple-element.277), kind=kOutput, calls=%fused_computation.5.clone.1 | convolution fusion | flops 403177472 | bytes 4194368 | tf_op jit(solution)/shard_map/while/body/eval_jaxpr/glpo,mglo,gl->mgp/dot_general | solution.py:59
  154.4 3.1 %fusion.37 = bf16[8,1,64,64]{3,1,2,0:T(2,128)(2,1)S(1)} fusion(f32[8,8,1,1]{1,2,3,0:T(1,128)S(1)} %copy.57, f32[64,8,8,64]{3,0,2,1:T(8,128)S(1)} %convolution_bitcast_fusion.2), kind=kOutput, calls=%fused_computation.3.clone.1 | convolution fusion | flops 3145728 | bytes 1114368 | tf_op jit(solution)/shard_map/while/body/eval_jaxpr/glpo,mglo,gl->mgp/dot_general | solution.py:59
  157.5 0.2 copy.59
  157.7 0.1 reshape.157
  157.9 0.1 reshape.156
  158.0 2.0 gather_fusion
  159.9 0.9 constant_dynamic-slice_fusion.2
  160.9 0.1 copy.58
  161.0 2.4 %fusion.36 = f32[8,8,128,64]{2,3,1,0:T(8,128)} fusion(f32[64,8,64,1]{0,2,3,1:T(8,128)S(1)} %bitcast.85, bf16[8,8,64,128]{3,2,1,0:T(8,128)(2,1)S(1)} %bitcast.83, pred[8,8]{1,0:T(8,128)(4,1)S(1)} %get-tuple-element.277), kind=kOutput, calls=%fused_computation.6.clone.1 | convolution fusion | flops 403177472 | bytes 3276864 | tf_op jit(solution)/shard_map/while/body/eval_jaxpr/mgp,mglo->glpo/dot_general | solution.py:58
  163.4 2.0 gather_fusion.1
  165.4 3.4 %convolution_bitcast_fusion.2 = f32[64,8,8,64]{3,0,2,1:T(8,128)S(1)} fusion(f32[8,8,128,64]{2,3,1,0:T(8,128)} %fusion.36, bf16[8,8,64,128]{3,2,1,0:T(8,128)(2,1)S(1)} %bitcast.84, pred[8,8]{1,0:T(8,128)(4,1)S(1)} %get-tuple-element.277), kind=kOutput, calls=%fused_computation.5.clone.1 | convolution fusion | flops 403177472 | bytes 4194368 | tf_op jit(solution)/shard_map/while/body/eval_jaxpr/glpo,mglo,gl->mgp/dot_general | solution.py:59
  169.0 3.1 %fusion.37 = bf16[8,1,64,64]{3,1,2,0:T(2,128)(2,1)S(1)} fusion(f32[8,8,1,1]{1,2,3,0:T(1,128)S(1)} %copy.57, f32[64,8,8,64]{3,0,2,1:T(8,128)S(1)} %convolution_bitcast_fusion.2), kind=kOutput, calls=%fused_computation.3.clone.1 | convolution fusion | flops 3145728 | bytes 1114368 | tf_op jit(solution)/shard_map/while/body/eval_jaxpr/glpo,mglo,gl->mgp/dot_general | solution.py:59
  172.1 0.2 copy.59
  172.2 0.1 reshape.157
  172.4 0.1 reshape.156
  172.5 2.0 gather_fusion
  174.5 0.9 constant_dynamic-slice_fusion.2
  175.4 0.1 copy.58
  175.6 2.4 %fusion.36 = f32[8,8,128,64]{2,3,1,0:T(8,128)} fusion(f32[64,8,64,1]{0,2,3,1:T(8,128)S(1)} %bitcast.85, bf16[8,8,64,128]{3,2,1,0:T(8,128)(2,1)S(1)} %bitcast.83, pred[8,8]{1,0:T(8,128)(4,1)S(1)} %get-tuple-element.277), kind=kOutput, calls=%fused_computation.6.clone.1 | convolution fusion | flops 403177472 | bytes 3276864 | tf_op jit(solution)/shard_map/while/body/eval_jaxpr/mgp,mglo->glpo/dot_general | solution.py:58
  178.0 2.0 gather_fusion.1
  179.9 3.4 %convolution_bitcast_fusion.2 = f32[64,8,8,64]{3,0,2,1:T(8,128)S(1)} fusion(f32[8,8,128,64]{2,3,1,0:T(8,128)} %fusion.36, bf16[8,8,64,128]{3,2,1,0:T(8,128)(2,1)S(1)} %bitcast.84, pred[8,8]{1,0:T(8,128)(4,1)S(1)} %get-tuple-element.277), kind=kOutput, calls=%fused_computation.5.clone.1 | convolution fusion | flops 403177472 | bytes 4194368 | tf_op jit(solution)/shard_map/while/body/eval_jaxpr/glpo,mglo,gl->mgp/dot_general | solution.py:59
  183.5 3.1 %fusion.37 = bf16[8,1,64,64]{3,1,2,0:T(2,128)(2,1)S(1)} fusion(f32[8,8,1,1]{1,2,3,0:T(1,128)S(1)} %copy.57, f32[64,8,8,64]{3,0,2,1:T(8,128)S(1)} %convolution_bitcast_fusion.2), kind=kOutput, calls=%fused_computation.3.clone.1 | convolution fusion | flops 3145728 | bytes 1114368 | tf_op jit(solution)/shard_map/while/body/eval_jaxpr/glpo,mglo,gl->mgp/dot_general | solution.py:59
  186.6 0.2 copy.59
  186.8 0.1 reshape.157
  187.0 1.2 fusion.13
  188.2 0.5 copy.38
  188.8 32.7 %all_to_all.32 = f32[64,1,2048]{2,1,0:T(1,128)S(1)} all-to-all(f32[64,1,2048]{2,1,0:T(1,128)S(1)} %copy.38), channel_id=1, replica_groups=mesh['slab'=64,'obs'=8] {'slab'}, dimensions={0} | all-to-all | bytes 1048576 | tf_op jit(solution)/shard_map/all_to_all | solution.py:94
  221.4 0.8 copy.69
  (40 shorter events, 1.0 us)
Async XLA Ops:
  6.5 32.5 %all-to-all-start = ((f32[1,64,2048]{2,0,1:T(1,128)}), f32[1,64,2048]{2,0,1:T(1,128)S(1)}, u32[]{:S(2)}, u32[]{:S(2)}) async-start(f32[1,64,2048]{2,0,1:T(1,128)} %bitcast.93), calls=%async_computation | async-start | bytes 1048576 | tf_op jit(solution)/shard_map/all_to_all | solution.py:77
  21.4 60.4 %all-gather.3.cloned.1.call-start = ((), (), s32[]{:S(2)}) async-start(), calls=%async_computation.2 | async-start | bytes 2359296 | tf_op jit(solution)/shard_map/all_gather | solution.py:41
  39.1 0.8 copy-start
  40.1 4.3 %copy-start.2 = (f32[1,1024]{1,0:T(1,128)S(1)}, f32[1,1024]{1,0:T(1,128)}, u32[]{:S(2)}) copy-start(f32[1,1024]{1,0:T(1,128)} %param.15) | copy-start | bytes 12292
  40.1 4.3 %copy-start.1 = (f32[1,1024]{1,0:T(1,128)S(1)}, f32[1,1024]{1,0:T(1,128)}, u32[]{:S(2)}) copy-start(f32[1,1024]{1,0:T(1,128)} %param.14) | copy-start | bytes 12292
  40.1 6.7 %copy-start.3 = (s32[1,32,8]{1,2,0:T(8,128)S(1)}, s32[1,32,8]{1,2,0:T(8,128)}, u32[]{:S(2)}) copy-start(s32[1,32,8]{1,2,0:T(8,128)} %param.18) | copy-start | bytes 3076
  40.1 6.8 %copy-start.4 = (f32[1,32,8]{1,2,0:T(8,128)S(1)}, f32[1,32,8]{1,2,0:T(8,128)}, u32[]{:S(2)}) copy-start(f32[1,32,8]{1,2,0:T(8,128)} %param.19) | copy-start | bytes 3076
  46.1 79.9 %all-gather.5.cloned.1.call-start = ((), (), s32[]{:S(2)}) async-start(), calls=%async_computation.3 | async-start | bytes 2359296 | tf_op jit(solution)/shard_map/all_gather | solution.py:40
Sparse Core Ops, SparseCore 0:
  46.2 35.5 all-gather.2
  83.8 42.0 all-gather.4
where the time goes:
time: 230 us; the launch traced here: 229 us
  waiting for transfers between devices  90.7 us (39%)
  matrix products  35.7 us (16%)
  local copies, waits for them, and re-layouts  33.8 us (15%)
  blocking collectives  32.7 us (14%)
  starting transfers between devices  14.9 us (6%)
  between operations  14.2 us (6%)
  other arithmetic  6.66 us (3%)
    all_gather x1, waiting for transfers between devices, compute_increment(): lax.all_gather(prior_low, 'obs', axis=1, tiled=True)  41.5 us
    all_gather x1, waiting for transfers between devices, compute_increment(): lax.all_gather(gain_input, 'obs', axis=1, tiled=True)  33.9 us
    all_to_all x1, blocking collectives, local(): lax.all_to_all(analysis, 'slab', split_axis=0, concat_axis=1, tiled=True)  32.7 us
    dot_general x8, matrix products, one_group(): jnp.einsum('glpo,mglo,gl->mgp', covariance, picked_gain, scales, precisio...  26.2 us
    all_to_all x1, starting transfers between devices, local(): lax.all_to_all(background_members, 'slab', split_axis=1, concat_axis=0, t...  14.8 us
    all_to_all x1, waiting for transfers between devices, local(): lax.all_to_all(background_members, 'slab', split_axis=1, concat_axis=0, t...  14.5 us
    dot_general x4, matrix products, one_group(): jnp.einsum('mgp,mglo->glpo', local_dev, picked_prior, precision=highest)  9.56 us
    gather x4, local copies, waits for them, and re-layouts, one_group(): picked_prior = jnp.take(all_prior, chosen, axis=1).astype(jnp.float32)  7.9 us
  transfers between devices with their start and end apart: 3, of which 3 were waited for; matrix products, arithmetic and copies ran while one was open for 3% of the time, Pallas kernels for 0%

commit v1 on v0

--- a/solution.py
+++ b/solution.py
@@ -37,7 +37,9 @@
     block_links = coupling_listing[0]
     factor = taper_factors[0] / (members - 1)
     gathered = (
-        lax.all_gather(prior_low, "obs", axis=1, tiled=True),
+        jnp.concatenate(
+            lax.all_to_all(jnp.stack([prior_low] * lax.axis_size("obs")), "obs", 0, 0), axis=1
+        ),
         lax.all_gather(gain_input, "obs", axis=1, tiled=True),
     )
     all_prior = gathered[0].reshape(members, -1, OB)

time: 230 us -> 197 us (0.86)
  waiting for transfers between devices: 90.7 us -> 62.1 us
  blocking collectives: 32.7 us -> 25.3 us
  starting transfers between devices: 14.9 us -> 21.7 us
    all_gather x1 -> x0, waiting for transfers between devices: 41.5 us -> none  [compute_increment(): lax.all_gather(prior_low, 'obs', axis=1, tiled=True)]
    all_gather x1, waiting for transfers between devices: 33.9 us -> 47.6 us  [compute_increment(): lax.all_gather(gain_input, 'obs', axis=1, tiled=True)]
    all_to_all x1, blocking collectives: 32.7 us -> 25.3 us  [local(): lax.all_to_all(analysis, 'slab', split_axis=0, concat_axis=1, tiled=True)]
    all_to_all x0 -> x1, starting transfers between devices: none -> 6.82 us  [compute_increment(): lax.all_to_all(jnp.stack([prior_low] * lax.axis_size('obs')), 'obs', 0, 0)]
    dynamic_slice x8, local copies, waits for them, and re-layouts: 4.16 us -> 0.55 us  [one_group(): lax.dynamic_slice_in_dim(deviation, first_block * block_width, group_size...]
  transfers between devices with their start and end apart: 3 -> 3, of which waited for: 3 -> 2; matrix products, arithmetic and copies ran while one was open for 3% -> 3% of each run, Pallas kernels for 0% -> 0%
where the time goes in v1:
time: 197 us
  waiting for transfers between devices  62.1 us (32%)
  matrix products  35.7 us (18%)
  local copies, waits for them, and re-layouts  31.8 us (16%)
  blocking collectives  25.3 us (13%)
  starting transfers between devices  21.7 us (11%)
  between operations  14.2 us (7%)
  other arithmetic  5.32 us (3%)
    all_gather x1, waiting for transfers between devices, compute_increment(): lax.all_gather(gain_input, 'obs', axis=1, tiled=True)  47.6 us
    dot_general x8, matrix products, one_group(): jnp.einsum('glpo,mglo,gl->mgp', covariance, picked_gain, scales, precisio...  26.2 us
    all_to_all x1, blocking collectives, local(): lax.all_to_all(analysis, 'slab', split_axis=0, concat_axis=1, tiled=True)  25.3 us
    all_to_all x1, starting transfers between devices, local(): lax.all_to_all(background_members, 'slab', split_axis=1, concat_axis=0, t...  14.8 us
    all_to_all x1, waiting for transfers between devices, local(): lax.all_to_all(background_members, 'slab', split_axis=1, concat_axis=0, t...  14.5 us
    dot_general x4, matrix products, one_group(): jnp.einsum('mgp,mglo->glpo', local_dev, picked_prior, precision=highest)  9.54 us
    gather x4, local copies, waits for them, and re-layouts, one_group(): picked_prior = jnp.take(all_prior, chosen, axis=1).astype(jnp.float32)  8.2 us
    gather x4, local copies, waits for them, and re-layouts, one_group(): picked_gain = jnp.take(all_gain, chosen, axis=1).astype(jnp.float32)  7.89 us
  transfers between devices with their start and end apart: 3, of which 2 were waited for; matrix products, arithmetic and copies ran while one was open for 3% of the time, Pallas kernels for 0%

profile of v1, /device:TPU:1, one launch (start us, length us, event | category | flops | bytes accessed | tf_op | source)
XLA Modules:
  0.0 196.6 jit_solution(2773102462150293254)
XLA Ops:
  6.5 14.8 %all-to-all-start = ((f32[1,64,2048]{2,0,1:T(1,128)}), f32[1,64,2048]{2,0,1:T(1,128)S(1)}, u32[]{:S(2)}, u32[]{:S(2)}) async-start(f32[1,64,2048]{2,0,1:T(1,128)} %bitcast.93), calls=%async_computation | async-start | bytes 1048576 | tf_op jit(solution)/shard_map/all_to_all | solution.py:79
  22.1 1.1 copy.43
  23.1 0.7 iota_compare_fusion
  23.8 0.7 compare_select_fusion.1
  24.5 14.5 %all-to-all-done = f32[1,64,2048]{2,0,1:T(1,128)S(1)} async-done(((f32[1,64,2048]{2,0,1:T(1,128)}), f32[1,64,2048]{2,0,1:T(1,128)S(1)}, u32[]{:S(2)}, u32[]{:S(2)}) %all-to-all-start) | async-done | bytes 524320 | tf_op jit(solution)/shard_map/all_to_all | solution.py:79
  39.1 0.2 copy.63
  39.2 0.6 copy-done
  39.9 0.2 copy.44
  40.1 2.8 %gather_fusion.2 = f32[1024,64]{1,0:T(8,128)S(1)} fusion(f32[64,2048]{0,1:T(8,128)S(1)} %copy.44, s32[1024]{0:T(1024)S(1)} %broadcast_clamp_fusion), kind=kCustom, calls=%fused_computation.2 | custom fusion | bytes 528384 | tf_op jit(solution)/shard_map/jit(_take)/gather | solution.py:28
  42.9 0.4 select_reduce_fusion
  43.3 0.5 fusion.18
  43.8 1.6 fusion.17
  45.5 0.1 copy.45
  45.6 1.1 stack.2
  46.7 6.8 %all-to-all-start.1 = ((bf16[8,64,1024]{2,1,0:T(8,128)(2,1)}), bf16[8,64,1024]{2,1,0:T(8,128)(2,1)S(1)}, u32[]{:S(2)}, u32[]{:S(2)}) async-start(bf16[8,64,1024]{2,1,0:T(8,128)(2,1)} %stack.2), calls=%async_computation.1 | async-start | bytes 2097152 | tf_op jit(solution)/shard_map/all_to_all | solution.py:41
  53.6 0.1 copy.42
  53.8 47.6 %all-gather.2.cloned.1.call-done = bf16[64,8192]{0,1:T(8,128)(2,1)} async-done(((bf16[64,1024]{0,1:T(8,128)(2,1)}), bf16[64,8192]{0,1:T(8,128)(2,1)}) %all-gather.2.cloned.1.call-update) | async-done | bytes 1048592 | tf_op jit(solution)/shard_map/all_gather | solution.py:43
  101.3 2.7 %copy.47 = bf16[64,64,128]{2,0,1:T(8,128)(2,1)} copy(bf16[64,64,128]{0,2,1:T(8,128)(2,1)} %bitcast.91) | data formatting | bytes 2097152 | tf_op jit(solution)/shard_map/while | solution.py:65
  104.0 0.6 copy.46
  104.6 0.5 reshape_reshape.3
  105.1 1.7 copy.48
  106.8 55.1 %while.15 = (s32[]{:T(128)}, bf16[64,2048]{1,0:T(8,128)(2,1)S(1)}, s32[32,8]{1,0:T(8,128)S(1)}, bf16[64,64,128]{2,0,1:T(8,128)(2,1)}, bf16[64,64,128]{2,0,1:T(8,...) while((s32[]{:T(128)}, bf16[64,2048]{1,0:T(8,128)(2,1)S(1)}, ...), condition=%wide.region_4.6_spmd, body=%wide.region_3.5_spmd.sunk | while | flops 809502080 | bytes 17898976 | solution.py:65
  106.8 0.1 reshape.176
  106.9 2.0 %gather_fusion = bf16[64,64,128]{2,1,0:T(8,128)(2,1)S(1)} fusion(bf16[64,64,128]{2,0,1:T(8,128)(2,1)} %get-tuple-element.315, s32[1024]{0:T(1024)S(1)} %pad_clamp_fusion.2), kind=kCustom, calls=%fused_computation.1.clone.clone.1 | custom fusion | bytes 2097408 | tf_op jit(solution)/shard_map/while/body/eval_jaxpr/jit(_take)/gather | solution.py:58
  109.0 0.1 copy.70
  109.1 2.4 %fusion.36 = f32[8,8,128,64]{2,3,1,0:T(8,128)} fusion(f32[64,8,64,1]{0,2,3,1:T(8,128)S(1)} %bitcast.85, bf16[8,8,64,128]{3,2,1,0:T(8,128)(2,1)S(1)} %bitcast.83, pred[8,8]{1,0:T(8,128)(4,1)S(1)} %get-tuple-element.284), kind=kOutput, calls=%fused_computation.6.clone.1 | convolution fusion | flops 403177472 | bytes 3276864 | tf_op jit(solution)/shard_map/while/body/eval_jaxpr/mgp,mglo->glpo/dot_general | solution.py:60
  111.5 2.0 %gather_fusion.1 = bf16[64,64,128]{2,1,0:T(8,128)(2,1)S(1)} fusion(bf16[64,64,128]{2,0,1:T(8,128)(2,1)} %get-tuple-element.314, s32[1024]{0:T(1024)S(1)} %pad_clamp_fusion.2), kind=kCustom, calls=%fused_computation.clone.clone.1 | custom fusion | bytes 2097408 | tf_op jit(solution)/shard_map/while/body/eval_jaxpr/jit(_take)/gather | solution.py:59
  113.5 3.4 %convolution_bitcast_fusion.2 = f32[64,8,8,64]{3,0,2,1:T(8,128)S(1)} fusion(f32[8,8,128,64]{2,3,1,0:T(8,128)} %fusion.36, bf16[8,8,64,128]{3,2,1,0:T(8,128)(2,1)S(1)} %bitcast.84, pred[8,8]{1,0:T(8,128)(4,1)S(1)} %get-tuple-element.284), kind=kOutput, calls=%fused_computation.5.clone.1 | convolution fusion | flops 403177472 | bytes 4194368 | tf_op jit(solution)/shard_map/while/body/eval_jaxpr/glpo,mglo,gl->mgp/dot_general | solution.py:61
  117.0 0.1 dynamic-slice_bitcast_fusion.2
  117.1 3.1 %fusion.37 = bf16[8,1,64,64]{3,1,2,0:T(2,128)(2,1)S(1)} fusion(f32[8,8,1,1]{1,2,3,0:T(1,128)S(1)} %copy.69, f32[64,8,8,64]{3,0,2,1:T(8,128)S(1)} %convolution_bitcast_fusion.2), kind=kOutput, calls=%fused_computation.3.clone.1 | convolution fusion | flops 3145728 | bytes 1114368 | tf_op jit(solution)/shard_map/while/body/eval_jaxpr/glpo,mglo,gl->mgp/dot_general | solution.py:61
  120.2 0.2 copy.71
  120.4 0.1 reshape.177
  120.6 0.1 reshape.176
  120.7 2.0 %gather_fusion = bf16[64,64,128]{2,1,0:T(8,128)(2,1)S(1)} fusion(bf16[64,64,128]{2,0,1:T(8,128)(2,1)} %get-tuple-element.315, s32[1024]{0:T(1024)S(1)} %pad_clamp_fusion.2), kind=kCustom, calls=%fused_computation.1.clone.clone.1 | custom fusion | bytes 2097408 | tf_op jit(solution)/shard_map/while/body/eval_jaxpr/jit(_take)/gather | solution.py:58
  122.8 0.1 copy.70
  122.9 2.4 %fusion.36 = f32[8,8,128,64]{2,3,1,0:T(8,128)} fusion(f32[64,8,64,1]{0,2,3,1:T(8,128)S(1)} %bitcast.85, bf16[8,8,64,128]{3,2,1,0:T(8,128)(2,1)S(1)} %bitcast.83, pred[8,8]{1,0:T(8,128)(4,1)S(1)} %get-tuple-element.284), kind=kOutput, calls=%fused_computation.6.clone.1 | convolution fusion | flops 403177472 | bytes 3276864 | tf_op jit(solution)/shard_map/while/body/eval_jaxpr/mgp,mglo->glpo/dot_general | solution.py:60
  125.3 2.0 %gather_fusion.1 = bf16[64,64,128]{2,1,0:T(8,128)(2,1)S(1)} fusion(bf16[64,64,128]{2,0,1:T(8,128)(2,1)} %get-tuple-element.314, s32[1024]{0:T(1024)S(1)} %pad_clamp_fusion.2), kind=kCustom, calls=%fused_computation.clone.clone.1 | custom fusion | bytes 2097408 | tf_op jit(solution)/shard_map/while/body/eval_jaxpr/jit(_take)/gather | solution.py:59
  127.3 3.4 %convolution_bitcast_fusion.2 = f32[64,8,8,64]{3,0,2,1:T(8,128)S(1)} fusion(f32[8,8,128,64]{2,3,1,0:T(8,128)} %fusion.36, bf16[8,8,64,128]{3,2,1,0:T(8,128)(2,1)S(1)} %bitcast.84, pred[8,8]{1,0:T(8,128)(4,1)S(1)} %get-tuple-element.284), kind=kOutput, calls=%fused_computation.5.clone.1 | convolution fusion | flops 403177472 | bytes 4194368 | tf_op jit(solution)/shard_map/while/body/eval_jaxpr/glpo,mglo,gl->mgp/dot_general | solution.py:61
  130.8 0.1 dynamic-slice_bitcast_fusion.2
  130.9 3.1 %fusion.37 = bf16[8,1,64,64]{3,1,2,0:T(2,128)(2,1)S(1)} fusion(f32[8,8,1,1]{1,2,3,0:T(1,128)S(1)} %copy.69, f32[64,8,8,64]{3,0,2,1:T(8,128)S(1)} %convolution_bitcast_fusion.2), kind=kOutput, calls=%fused_computation.3.clone.1 | convolution fusion | flops 3145728 | bytes 1114368 | tf_op jit(solution)/shard_map/while/body/eval_jaxpr/glpo,mglo,gl->mgp/dot_general | solution.py:61
  134.0 0.2 copy.71
  134.2 0.1 reshape.177
  134.4 0.1 reshape.176
  134.5 2.0 %gather_fusion = bf16[64,64,128]{2,1,0:T(8,128)(2,1)S(1)} fusion(bf16[64,64,128]{2,0,1:T(8,128)(2,1)} %get-tuple-element.315, s32[1024]{0:T(1024)S(1)} %pad_clamp_fusion.2), kind=kCustom, calls=%fused_computation.1.clone.clone.1 | custom fusion | bytes 2097408 | tf_op jit(solution)/shard_map/while/body/eval_jaxpr/jit(_take)/gather | solution.py:58
  136.6 0.1 copy.70
  136.7 2.4 %fusion.36 = f32[8,8,128,64]{2,3,1,0:T(8,128)} fusion(f32[64,8,64,1]{0,2,3,1:T(8,128)S(1)} %bitcast.85, bf16[8,8,64,128]{3,2,1,0:T(8,128)(2,1)S(1)} %bitcast.83, pred[8,8]{1,0:T(8,128)(4,1)S(1)} %get-tuple-element.284), kind=kOutput, calls=%fused_computation.6.clone.1 | convolution fusion | flops 403177472 | bytes 3276864 | tf_op jit(solution)/shard_map/while/body/eval_jaxpr/mgp,mglo->glpo/dot_general | solution.py:60
  139.1 2.0 %gather_fusion.1 = bf16[64,64,128]{2,1,0:T(8,128)(2,1)S(1)} fusion(bf16[64,64,128]{2,0,1:T(8,128)(2,1)} %get-tuple-element.314, s32[1024]{0:T(1024)S(1)} %pad_clamp_fusion.2), kind=kCustom, calls=%fused_computation.clone.clone.1 | custom fusion | bytes 2097408 | tf_op jit(solution)/shard_map/while/body/eval_jaxpr/jit(_take)/gather | solution.py:59
  141.1 3.4 %convolution_bitcast_fusion.2 = f32[64,8,8,64]{3,0,2,1:T(8,128)S(1)} fusion(f32[8,8,128,64]{2,3,1,0:T(8,128)} %fusion.36, bf16[8,8,64,128]{3,2,1,0:T(8,128)(2,1)S(1)} %bitcast.84, pred[8,8]{1,0:T(8,128)(4,1)S(1)} %get-tuple-element.284), kind=kOutput, calls=%fused_computation.5.clone.1 | convolution fusion | flops 403177472 | bytes 4194368 | tf_op jit(solution)/shard_map/while/body/eval_jaxpr/glpo,mglo,gl->mgp/dot_general | solution.py:61
  144.7 3.1 %fusion.37 = bf16[8,1,64,64]{3,1,2,0:T(2,128)(2,1)S(1)} fusion(f32[8,8,1,1]{1,2,3,0:T(1,128)S(1)} %copy.69, f32[64,8,8,64]{3,0,2,1:T(8,128)S(1)} %convolution_bitcast_fusion.2), kind=kOutput, calls=%fused_computation.3.clone.1 | convolution fusion | flops 3145728 | bytes 1114368 | tf_op jit(solution)/shard_map/while/body/eval_jaxpr/glpo,mglo,gl->mgp/dot_general | solution.py:61
  147.8 0.2 copy.71
  147.9 0.1 reshape.177
  148.2 0.1 reshape.176
  148.3 2.0 %gather_fusion = bf16[64,64,128]{2,1,0:T(8,128)(2,1)S(1)} fusion(bf16[64,64,128]{2,0,1:T(8,128)(2,1)} %get-tuple-element.315, s32[1024]{0:T(1024)S(1)} %pad_clamp_fusion.2), kind=kCustom, calls=%fused_computation.1.clone.clone.1 | custom fusion | bytes 2097408 | tf_op jit(solution)/shard_map/while/body/eval_jaxpr/jit(_take)/gather | solution.py:58
  150.4 0.1 copy.70
  150.5 2.4 %fusion.36 = f32[8,8,128,64]{2,3,1,0:T(8,128)} fusion(f32[64,8,64,1]{0,2,3,1:T(8,128)S(1)} %bitcast.85, bf16[8,8,64,128]{3,2,1,0:T(8,128)(2,1)S(1)} %bitcast.83, pred[8,8]{1,0:T(8,128)(4,1)S(1)} %get-tuple-element.284), kind=kOutput, calls=%fused_computation.6.clone.1 | convolution fusion | flops 403177472 | bytes 3276864 | tf_op jit(solution)/shard_map/while/body/eval_jaxpr/mgp,mglo->glpo/dot_general | solution.py:60
  152.9 2.0 %gather_fusion.1 = bf16[64,64,128]{2,1,0:T(8,128)(2,1)S(1)} fusion(bf16[64,64,128]{2,0,1:T(8,128)(2,1)} %get-tuple-element.314, s32[1024]{0:T(1024)S(1)} %pad_clamp_fusion.2), kind=kCustom, calls=%fused_computation.clone.clone.1 | custom fusion | bytes 2097408 | tf_op jit(solution)/shard_map/while/body/eval_jaxpr/jit(_take)/gather | solution.py:59
  154.8 3.4 %convolution_bitcast_fusion.2 = f32[64,8,8,64]{3,0,2,1:T(8,128)S(1)} fusion(f32[8,8,128,64]{2,3,1,0:T(8,128)} %fusion.36, bf16[8,8,64,128]{3,2,1,0:T(8,128)(2,1)S(1)} %bitcast.84, pred[8,8]{1,0:T(8,128)(4,1)S(1)} %get-tuple-element.284), kind=kOutput, calls=%fused_computation.5.clone.1 | convolution fusion | flops 403177472 | bytes 4194368 | tf_op jit(solution)/shard_map/while/body/eval_jaxpr/glpo,mglo,gl->mgp/dot_general | solution.py:61
  158.5 3.1 %fusion.37 = bf16[8,1,64,64]{3,1,2,0:T(2,128)(2,1)S(1)} fusion(f32[8,8,1,1]{1,2,3,0:T(1,128)S(1)} %copy.69, f32[64,8,8,64]{3,0,2,1:T(8,128)S(1)} %convolution_bitcast_fusion.2), kind=kOutput, calls=%fused_computation.3.clone.1 | convolution fusion | flops 3145728 | bytes 1114368 | tf_op jit(solution)/shard_map/while/body/eval_jaxpr/glpo,mglo,gl->mgp/dot_general | solution.py:61
  161.6 0.2 copy.71
  161.7 0.1 reshape.177
  161.9 1.2 fusion.13
  163.1 0.5 copy.50
  163.7 25.3 %all_to_all.37 = f32[64,1,2048]{2,1,0:T(1,128)S(1)} all-to-all(f32[64,1,2048]{2,1,0:T(1,128)S(1)} %copy.50), channel_id=1, replica_groups=mesh['slab'=64,'obs'=8] {'slab'}, dimensions={0} | all-to-all | bytes 1048576 | tf_op jit(solution)/shard_map/all_to_all | solution.py:96
  189.0 0.8 copy.81
  (59 shorter events, 0.9 us)
Async XLA Ops:
  6.5 32.5 %all-to-all-start = ((f32[1,64,2048]{2,0,1:T(1,128)}), f32[1,64,2048]{2,0,1:T(1,128)S(1)}, u32[]{:S(2)}, u32[]{:S(2)}) async-start(f32[1,64,2048]{2,0,1:T(1,128)} %bitcast.93), calls=%async_computation | async-start | bytes 1048576 | tf_op jit(solution)/shard_map/all_to_all | solution.py:79
  21.4 80.0 %all-gather.2.cloned.1.call-start = ((), (), s32[]{:S(2)}) async-start(), calls=%async_computation.3 | async-start | bytes 2359296 | tf_op jit(solution)/shard_map/all_gather | solution.py:43
  39.1 0.8 copy-start
  40.1 3.7 %copy-start.4 = (f32[1,1024]{1,0:T(1,128)S(1)}, f32[1,1024]{1,0:T(1,128)}, u32[]{:S(2)}) copy-start(f32[1,1024]{1,0:T(1,128)} %param.15) | copy-start | bytes 12292
  40.1 3.7 %copy-start.3 = (f32[1,1024]{1,0:T(1,128)S(1)}, f32[1,1024]{1,0:T(1,128)}, u32[]{:S(2)}) copy-start(f32[1,1024]{1,0:T(1,128)} %param.14) | copy-start | bytes 12292
  45.5 8.1 %copy-start.5 = (s32[1,32,8]{1,2,0:T(8,128)S(1)}, s32[1,32,8]{1,2,0:T(8,128)}, u32[]{:S(2)}) copy-start(s32[1,32,8]{1,2,0:T(8,128)} %param.18) | copy-start | bytes 3076
  45.5 8.2 %copy-start.6 = (f32[1,32,8]{1,2,0:T(8,128)S(1)}, f32[1,32,8]{1,2,0:T(8,128)}, u32[]{:S(2)}) copy-start(f32[1,32,8]{1,2,0:T(8,128)} %param.19) | copy-start | bytes 3076
  46.7 57.3 %all-to-all-start.1 = ((bf16[8,64,1024]{2,1,0:T(8,128)(2,1)}), bf16[8,64,1024]{2,1,0:T(8,128)(2,1)S(1)}, u32[]{:S(2)}, u32[]{:S(2)}) async-start(bf16[8,64,1024]{2,1,0:T(8,128)(2,1)} %stack.2), calls=%async_computation.1 | async-start | bytes 2097152 | tf_op jit(solution)/shard_map/all_to_all | solution.py:41
  106.8 4.7 %copy-start.1 = (f32[64,2048]{1,0:T(8,128)}, f32[64,2048]{1,0:T(8,128)S(1)}, u32[]{:S(2)}) copy-start(f32[64,2048]{1,0:T(8,128)S(1)} %get-tuple-element.316) | copy-start | bytes 1572868 | tf_op jit(solution)/shard_map/while
  117.0 3.6 %copy-start.2 = (f32[64,2048]{1,0:T(8,128)S(1)}, f32[64,2048]{1,0:T(8,128)}, u32[]{:S(2)}) copy-start(f32[64,2048]{1,0:T(8,128)} %copy-done.1) | copy-start | bytes 1572868 | tf_op jit(solution)/shard_map/while
  120.6 4.7 %copy-start.1 = (f32[64,2048]{1,0:T(8,128)}, f32[64,2048]{1,0:T(8,128)S(1)}, u32[]{:S(2)}) copy-start(f32[64,2048]{1,0:T(8,128)S(1)} %get-tuple-element.316) | copy-start | bytes 1572868 | tf_op jit(solution)/shard_map/while
  130.7 3.6 %copy-start.2 = (f32[64,2048]{1,0:T(8,128)S(1)}, f32[64,2048]{1,0:T(8,128)}, u32[]{:S(2)}) copy-start(f32[64,2048]{1,0:T(8,128)} %copy-done.1) | copy-start | bytes 1572868 | tf_op jit(solution)/shard_map/while
  134.4 4.7 %copy-start.1 = (f32[64,2048]{1,0:T(8,128)}, f32[64,2048]{1,0:T(8,128)S(1)}, u32[]{:S(2)}) copy-start(f32[64,2048]{1,0:T(8,128)S(1)} %get-tuple-element.316) | copy-start | bytes 1572868 | tf_op jit(solution)/shard_map/while
  144.5 3.6 %copy-start.2 = (f32[64,2048]{1,0:T(8,128)S(1)}, f32[64,2048]{1,0:T(8,128)}, u32[]{:S(2)}) copy-start(f32[64,2048]{1,0:T(8,128)} %copy-done.1) | copy-start | bytes 1572868 | tf_op jit(solution)/shard_map/while
  148.1 4.7 %copy-start.1 = (f32[64,2048]{1,0:T(8,128)}, f32[64,2048]{1,0:T(8,128)S(1)}, u32[]{:S(2)}) copy-start(f32[64,2048]{1,0:T(8,128)S(1)} %get-tuple-element.316) | copy-start | bytes 1572868 | tf_op jit(solution)/shard_map/while
  158.3 3.6 %copy-start.2 = (f32[64,2048]{1,0:T(8,128)S(1)}, f32[64,2048]{1,0:T(8,128)}, u32[]{:S(2)}) copy-start(f32[64,2048]{1,0:T(8,128)} %copy-done.1) | copy-start | bytes 1572868 | tf_op jit(solution)/shard_map/while
Sparse Core Ops, SparseCore 0:
  45.6 55.6 all-gather.1
